TPU v7x, 512 devices: a whole 4x8x8 slice. The times are simulated.
512 devices in a mesh: seq: 64 (over z_hi, y, core), ch: 8 (over x, z_lo).
Axes of the slice: x: 4, y: 8, z: 8 (z_hi: 4, z_lo: 2; z = z_hi * 2 + z_lo), core: 2. Of those that a mesh axis runs over, the one named last changes fastest.
Arguments:
- inputs: bfloat16 [262144, 2048], P('seq', 'ch'), may hold values from -6 to 6
- first_factor: bfloat16 [512, 512], P('ch'), may hold values from -0.25 to 0.25
- twiddle: float32 [512, 512], P('seq'), may hold values from -4 to 4
- second_factor: bfloat16 [512, 512], P('ch'), may hold values from -0.25 to 0.25
- block_first: bfloat16 [64, 32, 32], P('ch'), may hold values from -1 to 1
- block_second: bfloat16 [32, 64, 64], P('ch'), may hold values from -0.75 to 0.75
Outputs:
- mixed_out: bfloat16 [262144, 2048], P('seq', 'ch')
All inputs are finite; a program needn't handle non-finite values.
Results may differ from a plain program's by a relative error of at most 0.007.
Values may be sent and summed in bfloat16 or wider, within the bound.
No kernel may reach another device: no remote copies, remote signals or barrier semaphores. Data moves between devices by JAX's collectives and lax.ppermute only.
A program may use at most 128 MiB of HBM per device.

v0:
```python
import jax
import jax.numpy as jnp
from jax import lax
from jax.sharding import PartitionSpec as P

BLOCK = 512


def local(inputs, first_factor, twiddle, second_factor, block_first, block_second):
    tok_rows, channels = inputs.shape
    outer_rows = tok_rows // BLOCK
    token_grid = inputs.reshape(outer_rows, BLOCK, channels)
    contract = (((1,), (1,)), ((), ()))
    first = lax.dot_general(
        lax.all_gather(first_factor, "ch", axis=0, tiled=True),
        token_grid,
        contract,
        preferred_element_type=jnp.float32,
    )
    full_second = lax.all_gather(second_factor, "ch", axis=0, tiled=True)
    twisted = (first * jnp.transpose(twiddle)[:, :, None]).astype(jnp.bfloat16)
    mixed = lax.dot_general(
        full_second,
        lax.all_to_all(twisted, "seq", split_axis=0, concat_axis=1, tiled=True),
        contract,
        preferred_element_type=jnp.float32,
    )
    second = mixed.astype(jnp.bfloat16)
    returned = lax.all_to_all(second, "seq", split_axis=0, concat_axis=1, tiled=True)
    gated = (token_grid.astype(jnp.float32) * returned.astype(jnp.float32)).astype(jnp.bfloat16)
    grouped = gated.reshape(tok_rows, block_first.shape[0], block_first.shape[2])
    block_mix = jnp.einsum(
        "amb,tab->mat", block_first, grouped, preferred_element_type=jnp.float32
    ).astype(jnp.bfloat16)
    result_rows = jnp.einsum(
        "mpa,mat->tmp",
        block_second,
        lax.all_to_all(block_mix, "ch", split_axis=0, concat_axis=1, tiled=True),
        preferred_element_type=jnp.float32,
    )
    return result_rows.reshape(tok_rows, channels).astype(jnp.bfloat16)


def solution(mesh):
    placed = (
        P("seq", "ch"),
        P("ch", None),
        P("seq", None),
        P("ch", None),
        P("ch", None, None),
        P("ch", None, None),
    )
    return jax.shard_map(
        local, mesh=mesh, in_specs=placed, out_specs=P("seq", "ch"), check_vma=False
    )
```

profile of v0, /device:TPU:41, one launch (start us, length us, event | category | flops | bytes accessed | tf_op | source)
XLA Modules:
  0.0 266.0 jit_solution(8618646083847221918)
XLA Ops:
  0.0 0.0 copy-start
  0.0 25.3 %all_gather.6 = bf16[512,512]{1,0:T(8,128)(2,1)S(1)} all-gather(bf16[64,512]{1,0:T(8,128)(2,1)} %param.7), channel_id=1, replica_groups=mesh['seq'=64,'ch'=8] {'ch'}, dimensions={0}, use_global_device_ids=true | all-gather | bytes 589824 | tf_op jit(solution)/shard_map/all_gather | solution.py:15
  25.3 3.1 %multiply_convert_fusion = bf16[512,8,256]{2,0,1:T(8,128)(2,1)S(1)} fusion(bf16[8,512,256]{2,1,0:T(8,128)(2,1)} %bitcast.44, f32[512,8]{0,1:T(8,128)} %bitcast.46, bf16[512,512]{1,0:T(8,128)(2,1)S(1)} %all_gather.6), kind=kOutput, calls=%fused_computation.6 | convolution fusion | flops 1075838976 | bytes 4734976 | tf_op jit(solution)/shard_map/dot_general | solution.py:14
  28.4 2.5 copy.30
  30.9 0.0 copy-start.3
  30.9 21.6 %all-to-all-start = ((bf16[512,8,256]{2,1,0:T(8,128)(2,1)}), bf16[512,8,256]{2,1,0:T(8,128)(2,1)S(1)}, u32[]{:S(2)}, u32[]{:S(2)}) async-start(bf16[512,8,256]{2,1,0:T(8,128)(2,1)} %copy.30), calls=%async_computation | async-start | bytes 4194304 | tf_op jit(solution)/shard_map/all_to_all | solution.py:24
  52.5 0.0 copy-done.3
  52.5 64.1 %all_gather.7 = bf16[512,512]{1,0:T(8,128)(2,1)S(1)} all-gather(bf16[64,512]{1,0:T(8,128)(2,1)S(1)} %copy-done.3), channel_id=1, replica_groups=mesh['seq'=64,'ch'=8] {'ch'}, dimensions={0}, use_global_device_ids=true | all-gather | bytes 589824 | tf_op jit(solution)/shard_map/all_gather | solution.py:20
  116.6 0.0 all-to-all-done
  116.6 2.6 convert_bitcast_fusion.1
  119.2 4.5 %copy.33 = bf16[512,8,256]{2,1,0:T(8,128)(2,1)} copy(bf16[512,8,256]{0,2,1:T(8,128)(2,1)} %convert_bitcast_fusion.1) | data formatting | bytes 4194304 | tf_op jit(solution)/shard_map/convert_element_type | solution.py:28
  123.7 22.9 %all-to-all-start.1 = ((bf16[512,8,256]{2,1,0:T(8,128)(2,1)}), bf16[512,8,256]{2,1,0:T(8,128)(2,1)S(1)}, u32[]{:S(2)}, u32[]{:S(2)}) async-start(bf16[512,8,256]{2,1,0:T(8,128)(2,1)} %copy.33), calls=%async_computation.1 | async-start | bytes 4194304 | tf_op jit(solution)/shard_map/all_to_all | solution.py:29
  146.6 4.1 %copy.29 = bf16[4096,256]{0,1:T(8,128)(2,1)} copy(bf16[4096,256]{1,0:T(8,128)(2,1)} %param.6) | data formatting | bytes 4194304 | tf_op args[0]
  150.7 50.4 %all-to-all-done.1 = bf16[512,8,256]{2,1,0:T(8,128)(2,1)S(1)} async-done(((bf16[512,8,256]{2,1,0:T(8,128)(2,1)}), bf16[512,8,256]{2,1,0:T(8,128)(2,1)S(1)}, u32[]{:S(2)}, u32[]{:S(2)}) %all-to-all-start.1) | async-done | bytes 2097184 | tf_op jit(solution)/shard_map/all_to_all | solution.py:29
  201.1 0.5 convert_bitcast_fusion
  201.6 2.3 copy.34
  204.0 10.9 %reshape.17 = f32[4096,8,32]{2,1,0:T(8,128)} reshape(f32[8,64,8,256]{3,2,1,0:T(8,128)} %copy.34) | data formatting | bytes 8388608 | tf_op jit(solution)/shard_map/convert_element_type | solution.py:30
  214.9 0.0 copy-start.1
  214.9 11.6 %copy.35 = f32[4096,8,32]{0,2,1:T(8,128)} copy(f32[4096,8,32]{2,1,0:T(8,128)} %reshape.17) | data formatting | bytes 8388608 | tf_op jit(solution)/shard_map/convert_element_type | solution.py:30
  226.4 0.0 copy-done
  226.4 0.0 copy-done.1
  226.4 2.9 %fusion = bf16[32,8,4096]{2,0,1:T(8,128)(2,1)S(1)} fusion(bf16[8,32,32]{2,1,0:T(8,128)(2,1)S(1)} %copy-done, f32[4096,8,32]{0,2,1:T(8,128)} %copy.35, bf16[4096,8,32]{0,2,1:T(8,128)(2,1)S(1)} %bitcast.43), kind=kOutput, calls=%fused_computation.2 | convolution fusion | flops 71303168 | bytes 8404992 | tf_op jit(solution)/shard_map/amb,tab->mat/dot_general | solution.py:32
  229.3 1.2 copy.36
  230.5 0.0 copy-start.2
  230.5 32.3 %all_to_all.45 = bf16[32,8,4096]{2,1,0:T(8,128)(2,1)S(1)} all-to-all(bf16[32,8,4096]{2,1,0:T(8,128)(2,1)S(1)} %copy.36), channel_id=1, replica_groups=mesh['seq'=64,'ch'=8] {'ch'}, dimensions={0} | all-to-all | bytes 4194304 | tf_op jit(solution)/shard_map/all_to_all | solution.py:38
  262.8 0.0 copy-done.2
  262.8 0.7 convolution_convert_fusion
  263.5 2.5 copy.38
Async XLA Ops:
  0.0 226.4 %copy-start = (bf16[8,32,32]{2,1,0:T(8,128)(2,1)S(1)}, bf16[8,32,32]{2,1,0:T(8,128)(2,1)}, u32[]{:S(2)}) copy-start(bf16[8,32,32]{2,1,0:T(8,128)(2,1)} %param.10) | copy-start | bytes 49156
  30.9 21.6 %copy-start.3 = (bf16[64,512]{1,0:T(8,128)(2,1)S(1)}, bf16[64,512]{1,0:T(8,128)(2,1)}, u32[]{:S(2)}) copy-start(bf16[64,512]{1,0:T(8,128)(2,1)} %param.9) | copy-start | bytes 196612
  30.9 85.7 %all-to-all-start = ((bf16[512,8,256]{2,1,0:T(8,128)(2,1)}), bf16[512,8,256]{2,1,0:T(8,128)(2,1)S(1)}, u32[]{:S(2)}, u32[]{:S(2)}) async-start(bf16[512,8,256]{2,1,0:T(8,128)(2,1)} %copy.30), calls=%async_computation | async-start | bytes 4194304 | tf_op jit(solution)/shard_map/all_to_all | solution.py:24
  123.7 77.4 %all-to-all-start.1 = ((bf16[512,8,256]{2,1,0:T(8,128)(2,1)}), bf16[512,8,256]{2,1,0:T(8,128)(2,1)S(1)}, u32[]{:S(2)}, u32[]{:S(2)}) async-start(bf16[512,8,256]{2,1,0:T(8,128)(2,1)} %copy.33), calls=%async_computation.1 | async-start | bytes 4194304 | tf_op jit(solution)/shard_map/all_to_all | solution.py:29
  214.9 11.6 %copy-start.1 = (bf16[4096,256]{0,1:T(8,128)(2,1)S(1)}, bf16[4096,256]{0,1:T(8,128)(2,1)}, u32[]{:S(2)}) copy-start(bf16[4096,256]{0,1:T(8,128)(2,1)} %copy.29) | copy-start | bytes 6291460
  230.5 32.4 %copy-start.2 = (bf16[4,64,64]{2,1,0:T(8,128)(2,1)S(1)}, bf16[4,64,64]{2,1,0:T(8,128)(2,1)}, u32[]{:S(2)}) copy-start(bf16[4,64,64]{2,1,0:T(8,128)(2,1)} %param.11) | copy-start | bytes 98308
where the time goes:
time: 267 us; the launch traced here: 266 us
  blocking collectives  122 us (46%)
  waiting for transfers between devices  50.4 us (19%)
  starting transfers between devices  44.5 us (17%)
  local copies, waits for them, and re-layouts  39.5 us (15%)
  matrix products  9.27 us (3%)
    all_gather x1, blocking collectives, local(): full_second = lax.all_gather(second_factor, 'ch', axis=0, tiled=True)  64.1 us
    all_to_all x1, waiting for transfers between devices, local(): lax.all_to_all(second, 'seq', split_axis=0, concat_axis=1, tiled=True)  50.4 us
    all_to_all x1, blocking collectives, local(): lax.all_to_all(block_mix, 'ch', split_axis=0, concat_axis=1, tiled=True)  32.3 us
    all_gather x1, blocking collectives, local(): lax.all_gather(first_factor, 'ch', axis=0, tiled=True)  25.3 us
    convert_element_type x3, local copies, waits for them, and re-layouts, local(): returned.astype(jnp.float32)  24.8 us
    all_to_all x1, starting transfers between devices, local(): lax.all_to_all(second, 'seq', split_axis=0, concat_axis=1, tiled=True)  22.9 us
    all_to_all x1, starting transfers between devices, local(): lax.all_to_all(twisted, 'seq', split_axis=0, concat_axis=1, tiled=True)  21.6 us
  transfers between devices with their start and end apart: 2, of which 1 were waited for; matrix products, arithmetic and copies ran while one was open for 2% of the time, Pallas kernels for 0%

commit v1 on v0

--- a/solution.py
+++ b/solution.py
@@ -17,7 +17,9 @@
         contract,
         preferred_element_type=jnp.float32,
     )
-    full_second = lax.all_gather(second_factor, "ch", axis=0, tiled=True)
+    full_second = jnp.concatenate(
+        lax.all_to_all(jnp.stack([second_factor] * lax.axis_size("ch")), "ch", 0, 0), axis=0
+    )
     twisted = (first * jnp.transpose(twiddle)[:, :, None]).astype(jnp.bfloat16)
     mixed = lax.dot_general(
         full_second,

time: 267 us -> 250 us (0.936)
  starting transfers between devices: 44.5 us -> 15.3 us
  blocking collectives: 122 us -> 138 us
  matrix products: 9.27 us -> 6.36 us
    all_to_all x0 -> x1, blocking collectives: none -> 74.4 us  [local(): lax.all_to_all(twisted, 'seq', split_axis=0, concat_axis=1, tiled=True)]
    all_gather x1 -> x0, blocking collectives: 64.1 us -> none  [local(): full_second = lax.all_gather(second_factor, 'ch', axis=0, tiled=True)]
    all_to_all x1, starting transfers between devices: 21.6 us -> 5.83 us  [local(): lax.all_to_all(jnp.stack([second_factor] * lax.axis_size('ch')), 'ch', 0, 0)]
    all_to_all x1, starting transfers between devices: 22.9 us -> 9.49 us  [local(): lax.all_to_all(second, 'seq', split_axis=0, concat_axis=1, tiled=True)]
    all_to_all x1, blocking collectives: 32.3 us -> 35.8 us  [local(): lax.all_to_all(block_mix, 'ch', split_axis=0, concat_axis=1, tiled=True)]
    all_gather x1, blocking collectives: 25.3 us -> 28.2 us  [local(): lax.all_gather(first_factor, 'ch', axis=0, tiled=True)]
  transfers between devices with their start and end apart: 2 -> 2, of which waited for: 1 -> 1; matrix products, arithmetic and copies ran while one was open for 2% -> 3% of each run, Pallas kernels for 0% -> 0%
where the time goes in v1:
time: 250 us; the launch traced here: 249 us
  blocking collectives  138 us (55%)
  waiting for transfers between devices  49.5 us (20%)
  local copies, waits for them, and re-layouts  38.6 us (15%)
  starting transfers between devices  15.3 us (6%)
  matrix products  6.36 us (3%)
    all_to_all x1, blocking collectives, local(): lax.all_to_all(twisted, 'seq', split_axis=0, concat_axis=1, tiled=True)  74.4 us
    all_to_all x1, waiting for transfers between devices, local(): lax.all_to_all(second, 'seq', split_axis=0, concat_axis=1, tiled=True)  49.5 us
    all_to_all x1, blocking collectives, local(): lax.all_to_all(block_mix, 'ch', split_axis=0, concat_axis=1, tiled=True)  35.8 us
    all_gather x1, blocking collectives, local(): lax.all_gather(first_factor, 'ch', axis=0, tiled=True)  28.2 us
    convert_element_type x3, local copies, waits for them, and re-layouts, local(): returned.astype(jnp.float32)  24.8 us
    all_to_all x1, starting transfers between devices, local(): lax.all_to_all(second, 'seq', split_axis=0, concat_axis=1, tiled=True)  9.49 us
    all_to_all x1, starting transfers between devices, local(): lax.all_to_all(jnp.stack([second_factor] * lax.axis_size('ch')), 'ch', 0, 0)  5.83 us
  transfers between devices with their start and end apart: 2, of which 1 were waited for; matrix products, arithmetic and copies ran while one was open for 3% of the time, Pallas kernels for 0%

profile of v1, /device:TPU:41, one launch (start us, length us, event | category | flops | bytes accessed | tf_op | source)
XLA Modules:
  0.0 248.7 jit_solution(16546563243238842508)
XLA Ops:
  0.0 0.0 copy-start
  0.0 0.0 copy-start.2
  0.0 0.0 copy-start.4
  0.0 1.8 stack.2
  1.8 5.8 %all-to-all-start.1 = ((bf16[8,64,512]{2,1,0:T(8,128)(2,1)}), bf16[8,64,512]{2,1,0:T(8,128)(2,1)S(1)}, u32[]{:S(2)}, u32[]{:S(2)}) async-start(bf16[8,64,512]{2,1,0:T(8,128)(2,1)} %stack.2), calls=%async_computation.1 | async-start | bytes 1048576 | tf_op jit(solution)/shard_map/all_to_all | solution.py:21
  7.7 28.2 %all_gather.3 = bf16[512,512]{1,0:T(8,128)(2,1)S(1)} all-gather(bf16[64,512]{1,0:T(8,128)(2,1)} %param.7), channel_id=1, replica_groups=mesh['seq'=64,'ch'=8] {'ch'}, dimensions={0}, use_global_device_ids=true | all-gather | bytes 589824 | tf_op jit(solution)/shard_map/all_gather | solution.py:15
  35.9 0.0 copy-done.2
  35.9 0.0 copy-done.4
  35.9 1.5 multiply_convert_fusion
  37.3 1.2 copy.30
  38.5 0.0 all-to-all-done.1
  38.5 74.4 %all_to_all.50 = bf16[512,8,256]{2,1,0:T(8,128)(2,1)S(1)} all-to-all(bf16[512,8,256]{2,1,0:T(8,128)(2,1)S(1)} %copy.30), channel_id=1, replica_groups=mesh['seq'=64,'ch'=8] {'seq'}, dimensions={0} | all-to-all | bytes 4194304 | tf_op jit(solution)/shard_map/all_to_all | solution.py:26
  112.9 1.3 convert_bitcast_fusion.1
  114.3 3.1 %copy.33 = bf16[512,8,256]{2,1,0:T(8,128)(2,1)} copy(bf16[512,8,256]{0,2,1:T(8,128)(2,1)S(1)} %convert_bitcast_fusion.1) | data formatting | bytes 4194304 | tf_op jit(solution)/shard_map/convert_element_type | solution.py:30
  117.3 9.5 %all-to-all-start.2 = ((bf16[512,8,256]{2,1,0:T(8,128)(2,1)}), bf16[512,8,256]{2,1,0:T(8,128)(2,1)S(1)}, u32[]{:S(2)}, u32[]{:S(2)}) async-start(bf16[512,8,256]{2,1,0:T(8,128)(2,1)} %copy.33), calls=%async_computation.2 | async-start | bytes 4194304 | tf_op jit(solution)/shard_map/all_to_all | solution.py:31
  126.8 4.1 %copy.29 = bf16[4096,256]{0,1:T(8,128)(2,1)} copy(bf16[4096,256]{1,0:T(8,128)(2,1)} %param.6) | data formatting | bytes 4194304 | tf_op args[0]
  130.9 49.5 %all-to-all-done.2 = bf16[512,8,256]{2,1,0:T(8,128)(2,1)S(1)} async-done(((bf16[512,8,256]{2,1,0:T(8,128)(2,1)}), bf16[512,8,256]{2,1,0:T(8,128)(2,1)S(1)}, u32[]{:S(2)}, u32[]{:S(2)}) %all-to-all-start.2) | async-done | bytes 2097184 | tf_op jit(solution)/shard_map/all_to_all | solution.py:31
  180.4 0.5 convert_bitcast_fusion
  180.9 2.3 copy.34
  183.3 10.9 %reshape.23 = f32[4096,8,32]{2,1,0:T(8,128)} reshape(f32[8,64,8,256]{3,2,1,0:T(8,128)} %copy.34) | data formatting | bytes 8388608 | tf_op jit(solution)/shard_map/convert_element_type | solution.py:32
  194.2 0.0 copy-start.1
  194.2 11.6 %copy.35 = f32[4096,8,32]{0,2,1:T(8,128)} copy(f32[4096,8,32]{2,1,0:T(8,128)} %reshape.23) | data formatting | bytes 8388608 | tf_op jit(solution)/shard_map/convert_element_type | solution.py:32
  205.8 0.0 copy-done
  205.8 0.0 copy-done.1
  205.8 2.9 %fusion = bf16[32,8,4096]{2,0,1:T(8,128)(2,1)S(1)} fusion(bf16[8,32,32]{2,1,0:T(8,128)(2,1)S(1)} %copy-done, f32[4096,8,32]{0,2,1:T(8,128)} %copy.35, bf16[4096,8,32]{0,2,1:T(8,128)(2,1)S(1)} %bitcast.44), kind=kOutput, calls=%fused_computation.2 | convolution fusion | flops 71303168 | bytes 8404992 | tf_op jit(solution)/shard_map/amb,tab->mat/dot_general | solution.py:34
  208.7 1.2 copy.36
  209.8 0.0 copy-start.3
  209.8 35.8 %all_to_all.51 = bf16[32,8,4096]{2,1,0:T(8,128)(2,1)S(1)} all-to-all(bf16[32,8,4096]{2,1,0:T(8,128)(2,1)S(1)} %copy.36), channel_id=1, replica_groups=mesh['seq'=64,'ch'=8] {'ch'}, dimensions={0} | all-to-all | bytes 4194304 | tf_op jit(solution)/shard_map/all_to_all | solution.py:40
  245.6 0.0 copy-done.3
  245.6 0.7 convolution_convert_fusion
  246.3 2.5 copy.38
Async XLA Ops:
  0.0 205.8 %copy-start = (bf16[8,32,32]{2,1,0:T(8,128)(2,1)S(1)}, bf16[8,32,32]{2,1,0:T(8,128)(2,1)}, u32[]{:S(2)}) copy-start(bf16[8,32,32]{2,1,0:T(8,128)(2,1)} %param.10) | copy-start | bytes 49156
  0.0 35.9 %copy-start.2 = (bf16[4096,256]{1,0:T(8,128)(2,1)S(1)}, bf16[4096,256]{1,0:T(8,128)(2,1)}, u32[]{:S(2)}) copy-start(bf16[4096,256]{1,0:T(8,128)(2,1)} %param.6) | copy-start | bytes 6291460
  0.0 35.9 %copy-start.4 = (f32[8,512]{1,0:T(8,128)S(1)}, f32[8,512]{1,0:T(8,128)}, u32[]{:S(2)}) copy-start(f32[8,512]{1,0:T(8,128)} %param.8) | copy-start | bytes 49156
  1.8 36.7 %all-to-all-start.1 = ((bf16[8,64,512]{2,1,0:T(8,128)(2,1)}), bf16[8,64,512]{2,1,0:T(8,128)(2,1)S(1)}, u32[]{:S(2)}, u32[]{:S(2)}) async-start(bf16[8,64,512]{2,1,0:T(8,128)(2,1)} %stack.2), calls=%async_computation.1 | async-start | bytes 1048576 | tf_op jit(solution)/shard_map/all_to_all | solution.py:21
  117.3 63.0 %all-to-all-start.2 = ((bf16[512,8,256]{2,1,0:T(8,128)(2,1)}), bf16[512,8,256]{2,1,0:T(8,128)(2,1)S(1)}, u32[]{:S(2)}, u32[]{:S(2)}) async-start(bf16[512,8,256]{2,1,0:T(8,128)(2,1)} %copy.33), calls=%async_computation.2 | async-start | bytes 4194304 | tf_op jit(solution)/shard_map/all_to_all | solution.py:31
  194.2 11.6 %copy-start.1 = (bf16[4096,256]{0,1:T(8,128)(2,1)S(1)}, bf16[4096,256]{0,1:T(8,128)(2,1)}, u32[]{:S(2)}) copy-start(bf16[4096,256]{0,1:T(8,128)(2,1)} %copy.29) | copy-start | bytes 6291460
  209.8 35.8 %copy-start.3 = (bf16[4,64,64]{2,1,0:T(8,128)(2,1)S(1)}, bf16[4,64,64]{2,1,0:T(8,128)(2,1)}, u32[]{:S(2)}) copy-start(bf16[4,64,64]{2,1,0:T(8,128)(2,1)} %param.11) | copy-start | bytes 98308
